TPU v7x, 256 devices: a whole 4x4x8 slice. The times are simulated.
256 devices in a mesh: seq: 64 (over z_hi, y, x, core), tp: 4 (over z_lo).
Axes of the slice: x: 4, y: 4, z: 8 (z_hi: 2, z_lo: 4; z = z_hi * 4 + z_lo), core: 2. Of those that a mesh axis runs over, the one named last changes fastest.
Arguments:
- residual: bfloat16 [32768, 2048], P('seq', 'tp'), may hold values from -6 to 6
- norm_gain: float32 [2048], replicated, may hold values from 0.3 to 3
- query_weight: bfloat16 [2048, 1024], P(None, 'tp'), as said below
- key_weight: bfloat16 [2048, 1024], P(None, 'tp'), as said below
- value_weight: bfloat16 [2048, 1024], P(None, 'tp'), may hold values from -0.375 to 0.375
- out_weight: bfloat16 [1024, 2048], P('tp'), may hold values from -0.1875 to 0.1875
- segment_start: int32 [32768], P('seq'), may hold values from 0 to 32640, as said below
- token_valid: int32 [32768], P('seq'), may hold values from 0 to 1, as said below
- page_slot: int32 [256], P('seq'), may hold values from 4 to 511, as said below
Outputs:
- hidden: bfloat16 [32768, 2048], P('seq', 'tp')
- cache: bfloat16 [512, 128, 2048], P('seq', None, 'tp')
Inputs may be any that keep to these rules, and one draw needn't show every extreme that they name: `segment_start`: prompts start at multiples of 128 and are contiguous; each holds at most 8192 tokens and one holds exactly 8192. `token_valid`: zeros form a tail of the last page of a prompt; the first token of every prompt is 1. No two pages share a cache page; page_slot // 8 is the device that holds the page's tokens, or the next device when that one holds tokens of the same prompt. `query_weight`: independent entries whose scale falls as the inverse square root of 2048. `key_weight`: independent entries whose scale falls as the inverse square root of 2048.
All inputs are finite; a program needn't handle non-finite values.
Results may differ from a plain program's by a relative error of at most 0.02.
The roundings to bfloat16 on the way count: a program that leaves them out, or rounds other values in their place, can miss the bound.
Values may be sent and summed in bfloat16 or wider, within the bound.
No kernel may reach another device: no remote copies, remote signals or barrier semaphores. Data moves between devices by JAX's collectives and lax.ppermute only.
A program may use at most 128 MiB of HBM per device.

v0:
```python
import jax
import jax.numpy as jnp
from jax import lax
from jax.sharding import PartitionSpec as P

HD = 64
PAGE = 128
SPAN = 16
THETA = 130000.0
EPS = 1e-05


def passed_along(x, axis, by):
    count = lax.axis_size(axis)
    pairs = [(i, i + by) for i in range(count) if 0 <= i + by < count]
    return lax.ppermute(x, axis, pairs)


def rotate(inputs, positions):
    half_dim = inputs.shape[-1] // 2
    frequency = THETA ** (-2.0 * jnp.arange(half_dim, dtype=jnp.float32) / inputs.shape[-1])
    angles = positions.astype(jnp.float32)[:, None] * frequency[None, :]
    cosine = jnp.cos(angles)[:, None, :]
    sine_part = jnp.sin(angles)[:, None, :]
    front_half = inputs[..., :half_dim]
    back_half = inputs[..., half_dim:]
    return jnp.concatenate(
        [front_half * cosine - back_half * sine_part, back_half * cosine + front_half * sine_part],
        axis=-1,
    )


def body(
    residual,
    norm_gain,
    query_weight,
    key_weight,
    value_weight,
    out_weight,
    segment_start,
    token_valid,
    page_slot,
):
    row_count = residual.shape[0]
    local_heads = query_weight.shape[1] // HD
    gathered = lax.all_gather(residual, "tp", axis=1, tiled=True)
    widened = gathered.astype(jnp.float32)
    mean_sq = jnp.mean(widened * widened, axis=1, keepdims=True)
    normed = (widened * lax.rsqrt(mean_sq + EPS) * norm_gain[None, :]).astype(jnp.bfloat16)
    seq_rank = lax.axis_index("seq")
    first_row = seq_rank * row_count
    places = first_row + jnp.arange(row_count, dtype=jnp.int32)
    offsets = places - segment_start
    queries = jnp.dot(normed, query_weight, preferred_element_type=jnp.float32).reshape(
        row_count, local_heads, HD
    )
    queries = rotate(queries, offsets).astype(jnp.bfloat16)
    key_rot = jnp.dot(normed, key_weight, preferred_element_type=jnp.float32).reshape(
        row_count, local_heads, HD
    )
    key_rot = rotate(key_rot, offsets).astype(jnp.bfloat16)
    values = (
        jnp.dot(normed, value_weight, preferred_element_type=jnp.float32)
        .reshape(row_count, local_heads, HD)
        .astype(jnp.bfloat16)
    )
    packed = jnp.concatenate([key_rot[:, :, None, :], values[:, :, None, :]], axis=2).reshape(
        row_count, local_heads * 2 * HD
    )
    packed = jnp.where(token_valid[:, None] > 0, packed, jnp.zeros_like(packed))
    score_scale = HD ** (-0.5)
    out_cols = lax.all_to_all(out_weight, "tp", 1, 0, tiled=True)
    prev_slot = passed_along(page_slot, "seq", 1)

    def attend_block(running, incoming, allowed):
        row_max, norm_sum, weighted = running
        key_value = incoming.reshape(incoming.shape[0], local_heads, 2, HD)
        scores = (
            jnp.einsum(
                "qhd,khd->hqk", queries, key_value[:, :, 0, :], preferred_element_type=jnp.float32
            )
            * score_scale
        )
        block_max = jnp.max(jnp.where(allowed[None], scores, -1e30), axis=2)
        new_max = jnp.maximum(row_max, block_max)
        weights = jnp.where(allowed[None], jnp.exp(scores - new_max[:, :, None]), 0.0)
        shrink = jnp.exp(row_max - new_max)
        norm_sum = norm_sum * shrink + jnp.sum(weights, axis=2)
        update = jnp.einsum(
            "hqk,khd->qhd",
            weights.astype(jnp.bfloat16),
            key_value[:, :, 1, :],
            preferred_element_type=jnp.float32,
        )
        weighted = weighted * jnp.transpose(shrink)[:, :, None] + update
        return (new_max, norm_sum, weighted)

    local_pos = jnp.arange(row_count, dtype=jnp.int32)
    own_allowed = (
        ((first_row + local_pos)[None, :] >= segment_start[:, None])
        & (local_pos[None, :] <= local_pos[:, None])
        & (token_valid[None, :] > 0)
    )
    initial = (
        jnp.full((local_heads, row_count), -1e30, jnp.float32),
        jnp.zeros((local_heads, row_count), jnp.float32),
        jnp.zeros((row_count, local_heads, HD), jnp.float32),
    )
    carried = attend_block(initial, packed, own_allowed)

    def remote_absorb(running, incoming, step):
        key_places = first_row - step * row_count + local_pos
        allowed = key_places[None, :] >= segment_start[:, None]
        return attend_block(running, incoming, allowed)

    prev_block = passed_along(packed, "seq", 1)
    carried = remote_absorb(carried, prev_block, 1)
    reach_dev = min(SPAN, lax.axis_size("seq") // 2)

    def advance(step_index, carry_in):
        moving, running = carry_in
        moving = passed_along(moving, "seq", 1)
        running = remote_absorb(running, moving, step_index)
        return (moving, running)

    _, carried = lax.fori_loop(2, reach_dev + 1, advance, (prev_block, carried))
    row_max, norm_sum, weighted = carried
    attended = (
        (weighted / jnp.transpose(norm_sum)[:, :, None])
        .astype(jnp.bfloat16)
        .reshape(row_count, local_heads * HD)
    )
    tiles = page_slot.shape[0]
    slot_count = 2 * tiles
    base_slot = seq_rank * slot_count
    has_prev = seq_rank > 0
    cand_slot = jnp.concatenate([page_slot, jnp.where(has_prev, prev_slot, -1)]) - base_slot
    cand_pages = jnp.concatenate(
        [packed.reshape(tiles, PAGE, -1), prev_block.reshape(tiles, PAGE, -1)], axis=0
    )
    match = cand_slot[None, :] == jnp.arange(slot_count, dtype=jnp.int32)[:, None]
    pick = jnp.argmax(match.astype(jnp.int32), axis=1)
    found = jnp.any(match, axis=1)
    cache_pages = jnp.where(found[:, None, None], cand_pages[pick], jnp.zeros_like(cand_pages[:1]))
    attended_all = lax.all_gather(attended, "tp", axis=1, tiled=True)
    projected = jnp.dot(attended_all, out_cols, preferred_element_type=jnp.float32)
    hidden = (residual.astype(jnp.float32) + projected).astype(jnp.bfloat16)
    return (hidden, cache_pages)


def solution(mesh):
    return jax.shard_map(
        body,
        mesh=mesh,
        in_specs=(
            P("seq", "tp"),
            P(),
            P(None, "tp"),
            P(None, "tp"),
            P(None, "tp"),
            P("tp", None),
            P("seq"),
            P("seq"),
            P("seq"),
        ),
        out_specs=(P("seq", "tp"), P("seq", None, "tp")),
        check_vma=False,
    )
```

profile of v0, /device:TPU:1, one launch (start us, length us, event | category | flops | bytes accessed | tf_op | source)
XLA Modules:
  0.0 500.1 jit_solution(5178662731228044125)
XLA Ops:
  10.2 6.4 %all-to-all-start = ((bf16[256,4,512]{0,2,1:T(8,128)(2,1)}), bf16[256,4,512]{0,2,1:T(8,128)(2,1)S(1)}, u32[]{:S(2)}, u32[]{:S(2)}) async-start(bf16[256,4,512]{0,2,1:T(8,128)(2,1)} %bitcast.17), calls=%async_computation | async-start | bytes 2097152 | tf_op jit(solution)/shard_map/all_to_all | solution.py:72
  22.2 50.8 %all-gather.3.cloned.1.call-done = bf16[512,2048]{1,0:T(8,128)(2,1)} async-done(((bf16[512,512]{1,0:T(8,128)(2,1)}), bf16[512,2048]{1,0:T(8,128)(2,1)}) %all-gather.3.cloned.1.call-update) | async-done | bytes 2097168 | tf_op jit(solution)/shard_map/all_gather | solution.py:46
  83.7 5.1 %collective-permute-start.1 = (bf16[512,512]{0,1:T(8,128)(2,1)}, bf16[512,512]{0,1:T(8,128)(2,1)S(1)}, u32[]{:S(2)}, u32[]{:S(2)}) collective-permute-start(bf16[512,512]{0,1:T(8,128)(2,1)} %bitcast_select_fusion), channel_id=1, source_target_pairs={{0,4},{4,8},{8,12},{12,16},{16,20},{20,24},{24,28},{28,32},{32,36}... | collective-permute-start | bytes 1572872 | tf_op jit(solution)/shard_map/ppermute | solution.py:16
  102.8 220.3 %while.20 = (s32[]{:T(128)}, bf16[512,512]{0,1:T(8,128)(2,1)}, f32[4,512]{1,0:T(4,128)S(1)}, f32[4,512]{1,0:T(4,128)S(1)}, f32[512,4,64]{0,2,1:T(8,128)}, /*inde...) while((s32[]{:T(128)}, bf16[512,512]{0,1:T(8,128)(2,1)}, ...), condition=%wide.region_8.9_spmd.clone, body=%wide.region_5.8_spmd.clone.sunk | while | flops 280500736 | bytes 22943988 | solution.py:126
  102.8 4.3 collective-permute-start
  107.3 6.2 %collective-permute-done = bf16[512,512]{0,1:T(8,128)(2,1)S(1)} collective-permute-done((bf16[512,512]{0,1:T(8,128)(2,1)}, bf16[512,512]{0,1:T(8,128)(2,1)S(1)}, u32[]{:S(2)}, u32[]{:S(2)}) %collective-permute-start) | collective-permute-done | bytes 524320 | tf_op jit(solution)/shard_map/while/body/eval_jaxpr/ppermute | solution.py:16
  117.5 4.3 collective-permute-start
  122.0 6.2 %collective-permute-done = bf16[512,512]{0,1:T(8,128)(2,1)S(1)} collective-permute-done((bf16[512,512]{0,1:T(8,128)(2,1)}, bf16[512,512]{0,1:T(8,128)(2,1)S(1)}, u32[]{:S(2)}, u32[]{:S(2)}) %collective-permute-start) | collective-permute-done | bytes 524320 | tf_op jit(solution)/shard_map/while/body/eval_jaxpr/ppermute | solution.py:16
  132.1 4.3 collective-permute-start
  136.7 6.2 %collective-permute-done = bf16[512,512]{0,1:T(8,128)(2,1)S(1)} collective-permute-done((bf16[512,512]{0,1:T(8,128)(2,1)}, bf16[512,512]{0,1:T(8,128)(2,1)S(1)}, u32[]{:S(2)}, u32[]{:S(2)}) %collective-permute-start) | collective-permute-done | bytes 524320 | tf_op jit(solution)/shard_map/while/body/eval_jaxpr/ppermute | solution.py:16
  146.8 4.3 collective-permute-start
  151.4 6.2 %collective-permute-done = bf16[512,512]{0,1:T(8,128)(2,1)S(1)} collective-permute-done((bf16[512,512]{0,1:T(8,128)(2,1)}, bf16[512,512]{0,1:T(8,128)(2,1)S(1)}, u32[]{:S(2)}, u32[]{:S(2)}) %collective-permute-start) | collective-permute-done | bytes 524320 | tf_op jit(solution)/shard_map/while/body/eval_jaxpr/ppermute | solution.py:16
  161.5 4.3 collective-permute-start
  166.0 6.2 %collective-permute-done = bf16[512,512]{0,1:T(8,128)(2,1)S(1)} collective-permute-done((bf16[512,512]{0,1:T(8,128)(2,1)}, bf16[512,512]{0,1:T(8,128)(2,1)S(1)}, u32[]{:S(2)}, u32[]{:S(2)}) %collective-permute-start) | collective-permute-done | bytes 524320 | tf_op jit(solution)/shard_map/while/body/eval_jaxpr/ppermute | solution.py:16
  176.2 4.3 collective-permute-start
  180.7 6.2 %collective-permute-done = bf16[512,512]{0,1:T(8,128)(2,1)S(1)} collective-permute-done((bf16[512,512]{0,1:T(8,128)(2,1)}, bf16[512,512]{0,1:T(8,128)(2,1)S(1)}, u32[]{:S(2)}, u32[]{:S(2)}) %collective-permute-start) | collective-permute-done | bytes 524320 | tf_op jit(solution)/shard_map/while/body/eval_jaxpr/ppermute | solution.py:16
  190.9 4.3 collective-permute-start
  195.4 6.2 %collective-permute-done = bf16[512,512]{0,1:T(8,128)(2,1)S(1)} collective-permute-done((bf16[512,512]{0,1:T(8,128)(2,1)}, bf16[512,512]{0,1:T(8,128)(2,1)S(1)}, u32[]{:S(2)}, u32[]{:S(2)}) %collective-permute-start) | collective-permute-done | bytes 524320 | tf_op jit(solution)/shard_map/while/body/eval_jaxpr/ppermute | solution.py:16
  205.6 4.3 collective-permute-start
  210.1 6.2 %collective-permute-done = bf16[512,512]{0,1:T(8,128)(2,1)S(1)} collective-permute-done((bf16[512,512]{0,1:T(8,128)(2,1)}, bf16[512,512]{0,1:T(8,128)(2,1)S(1)}, u32[]{:S(2)}, u32[]{:S(2)}) %collective-permute-start) | collective-permute-done | bytes 524320 | tf_op jit(solution)/shard_map/while/body/eval_jaxpr/ppermute | solution.py:16
  220.3 4.3 collective-permute-start
  224.8 6.2 %collective-permute-done = bf16[512,512]{0,1:T(8,128)(2,1)S(1)} collective-permute-done((bf16[512,512]{0,1:T(8,128)(2,1)}, bf16[512,512]{0,1:T(8,128)(2,1)S(1)}, u32[]{:S(2)}, u32[]{:S(2)}) %collective-permute-start) | collective-permute-done | bytes 524320 | tf_op jit(solution)/shard_map/while/body/eval_jaxpr/ppermute | solution.py:16
  234.9 4.3 collective-permute-start
  239.5 6.2 %collective-permute-done = bf16[512,512]{0,1:T(8,128)(2,1)S(1)} collective-permute-done((bf16[512,512]{0,1:T(8,128)(2,1)}, bf16[512,512]{0,1:T(8,128)(2,1)S(1)}, u32[]{:S(2)}, u32[]{:S(2)}) %collective-permute-start) | collective-permute-done | bytes 524320 | tf_op jit(solution)/shard_map/while/body/eval_jaxpr/ppermute | solution.py:16
  249.6 4.3 collective-permute-start
  254.2 6.2 %collective-permute-done = bf16[512,512]{0,1:T(8,128)(2,1)S(1)} collective-permute-done((bf16[512,512]{0,1:T(8,128)(2,1)}, bf16[512,512]{0,1:T(8,128)(2,1)S(1)}, u32[]{:S(2)}, u32[]{:S(2)}) %collective-permute-start) | collective-permute-done | bytes 524320 | tf_op jit(solution)/shard_map/while/body/eval_jaxpr/ppermute | solution.py:16
  264.3 4.3 collective-permute-start
  268.8 6.2 %collective-permute-done = bf16[512,512]{0,1:T(8,128)(2,1)S(1)} collective-permute-done((bf16[512,512]{0,1:T(8,128)(2,1)}, bf16[512,512]{0,1:T(8,128)(2,1)S(1)}, u32[]{:S(2)}, u32[]{:S(2)}) %collective-permute-start) | collective-permute-done | bytes 524320 | tf_op jit(solution)/shard_map/while/body/eval_jaxpr/ppermute | solution.py:16
  283.5 6.2 %collective-permute-done = bf16[512,512]{0,1:T(8,128)(2,1)S(1)} collective-permute-done((bf16[512,512]{0,1:T(8,128)(2,1)}, bf16[512,512]{0,1:T(8,128)(2,1)S(1)}, u32[]{:S(2)}, u32[]{:S(2)}) %collective-permute-start) | collective-permute-done | bytes 524320 | tf_op jit(solution)/shard_map/while/body/eval_jaxpr/ppermute | solution.py:16
  298.2 6.2 %collective-permute-done = bf16[512,512]{0,1:T(8,128)(2,1)S(1)} collective-permute-done((bf16[512,512]{0,1:T(8,128)(2,1)}, bf16[512,512]{0,1:T(8,128)(2,1)S(1)}, u32[]{:S(2)}, u32[]{:S(2)}) %collective-permute-start) | collective-permute-done | bytes 524320 | tf_op jit(solution)/shard_map/while/body/eval_jaxpr/ppermute | solution.py:16
  312.9 6.2 %collective-permute-done = bf16[512,512]{0,1:T(8,128)(2,1)S(1)} collective-permute-done((bf16[512,512]{0,1:T(8,128)(2,1)}, bf16[512,512]{0,1:T(8,128)(2,1)S(1)}, u32[]{:S(2)}, u32[]{:S(2)}) %collective-permute-start) | collective-permute-done | bytes 524320 | tf_op jit(solution)/shard_map/while/body/eval_jaxpr/ppermute | solution.py:16
  332.5 157.5 %all-gather.5.cloned.1.call-done = bf16[512,1024]{0,1:T(8,128)(2,1)} async-done(((bf16[512,256]{0,1:T(8,128)(2,1)}), bf16[512,1024]{0,1:T(8,128)(2,1)}) %all-gather.5.cloned.1.call-update) | async-done | bytes 1048592 | tf_op jit(solution)/shard_map/all_gather | solution.py:145
  (272 shorter events, 120.6 us)
Async XLA Ops:
  7.2 68.1 %copy-start = (bf16[2048,256]{1,0:T(8,128)(2,1)S(1)}, bf16[2048,256]{1,0:T(8,128)(2,1)}, u32[]{:S(2)}) copy-start(bf16[2048,256]{1,0:T(8,128)(2,1)} %param.14) | copy-start | bytes 3145732
  7.2 9.5 %copy-start.10 = (s32[4]{0:T(128)S(1)}, s32[4]{0:T(128)}, u32[]{:S(2)}) copy-start(s32[4]{0:T(128)} %param.19) | copy-start | bytes 52
  7.2 13.5 %copy-start.9 = (s32[512]{0:T(512)S(1)}, s32[512]{0:T(512)}, u32[]{:S(2)}) copy-start(s32[512]{0:T(512)} %param.18) | copy-start | bytes 6148
  7.2 13.5 %copy-start.8 = (s32[512]{0:T(512)S(1)}, s32[512]{0:T(512)}, u32[]{:S(2)}) copy-start(s32[512]{0:T(512)} %param.17) | copy-start | bytes 6148
  7.2 68.1 %copy-start.12 = (f32[2048]{0:T(1024)S(1)}, f32[2048]{0:T(1024)}, u32[]{:S(2)}) copy-start(f32[2048]{0:T(1024)} %param.12) | copy-start | bytes 24580
  7.2 65.8 %all-gather.3.cloned.1.call-start = ((), (), s32[]{:S(2)}) async-start(), calls=%async_computation.1 | async-start | bytes 2621440 | tf_op jit(solution)/shard_map/all_gather | solution.py:46
  10.2 316.2 %all-to-all-start = ((bf16[256,4,512]{0,2,1:T(8,128)(2,1)}), bf16[256,4,512]{0,2,1:T(8,128)(2,1)S(1)}, u32[]{:S(2)}, u32[]{:S(2)}) async-start(bf16[256,4,512]{0,2,1:T(8,128)(2,1)} %bitcast.17), calls=%async_computation | async-start | bytes 2097152 | tf_op jit(solution)/shard_map/all_to_all | solution.py:72
  16.7 473.4 %all-gather.5.cloned.1.call-start = ((), (), s32[]{:S(2)}) async-start(), calls=%async_computation.2 | async-start | bytes 1310720 | tf_op jit(solution)/shard_map/all_gather | solution.py:145
  16.7 308.2 %collective-permute-start.2 = (s32[4]{0:T(128)S(1)}, s32[4]{0:T(128)}, u32[]{:S(2)}, u32[]{:S(2)}) collective-permute-start(s32[4]{0:T(128)S(1)} %copy-done.10), channel_id=1, source_target_pairs={{0,4},{4,8},{8,12},{12,16},{16,20},{20,24},{24,28},{28,32},{32,36}... | collective-permute-start | bytes 56 | tf_op jit(solution)/shard_map/ppermute | solution.py:16
  73.0 4.8 copy-start.1
  77.8 3.1 copy-start.11
  83.7 11.3 %collective-permute-start.1 = (bf16[512,512]{0,1:T(8,128)(2,1)}, bf16[512,512]{0,1:T(8,128)(2,1)S(1)}, u32[]{:S(2)}, u32[]{:S(2)}) collective-permute-start(bf16[512,512]{0,1:T(8,128)(2,1)} %bitcast_select_fusion), channel_id=1, source_target_pairs={{0,4},{4,8},{8,12},{12,16},{16,20},{20,24},{24,28},{28,32},{32,36}... | collective-permute-start | bytes 1572872 | tf_op jit(solution)/shard_map/ppermute | solution.py:16
  89.7 7.5 %copy-start.4 = (pred[512,512]{0,1:T(8,128)(4,1)S(1)}, pred[512,512]{0,1:T(8,128)(4,1)}, u32[]{:S(2)}) copy-start(pred[512,512]{0,1:T(8,128)(4,1)} %get-tuple-element.213) | copy-start | bytes 786436
  95.0 7.0 %copy-start.2 = (bf16[512,512]{0,1:T(8,128)(2,1)}, bf16[512,512]{0,1:T(8,128)(2,1)S(1)}, u32[]{:S(2)}) copy-start(bf16[512,512]{0,1:T(8,128)(2,1)S(1)} %collective-permute-done.1) | copy-start | bytes 1572868
  95.0 3.1 copy-start.7
  102.8 10.7 %collective-permute-start = (bf16[512,512]{0,1:T(8,128)(2,1)}, bf16[512,512]{0,1:T(8,128)(2,1)S(1)}, u32[]{:S(2)}, u32[]{:S(2)}) collective-permute-start(bf16[512,512]{0,1:T(8,128)(2,1)} %get-tuple-element.290), channel_id=1, source_target_pairs={{0,4},{4,8},{8,12},{12,16},{16,20},{20,24},{24,28},{28,32},{32,36}... | collective-permute-start | bytes 1572872 | tf_op jit(solution)/shard_map/while/body/eval_jaxpr/ppermute | solution.py:16
  113.5 1.9 copy-start.5
  117.5 10.7 %collective-permute-start = (bf16[512,512]{0,1:T(8,128)(2,1)}, bf16[512,512]{0,1:T(8,128)(2,1)S(1)}, u32[]{:S(2)}, u32[]{:S(2)}) collective-permute-start(bf16[512,512]{0,1:T(8,128)(2,1)} %get-tuple-element.290), channel_id=1, source_target_pairs={{0,4},{4,8},{8,12},{12,16},{16,20},{20,24},{24,28},{28,32},{32,36}... | collective-permute-start | bytes 1572872 | tf_op jit(solution)/shard_map/while/body/eval_jaxpr/ppermute | solution.py:16
  132.1 10.7 %collective-permute-start = (bf16[512,512]{0,1:T(8,128)(2,1)}, bf16[512,512]{0,1:T(8,128)(2,1)S(1)}, u32[]{:S(2)}, u32[]{:S(2)}) collective-permute-start(bf16[512,512]{0,1:T(8,128)(2,1)} %get-tuple-element.290), channel_id=1, source_target_pairs={{0,4},{4,8},{8,12},{12,16},{16,20},{20,24},{24,28},{28,32},{32,36}... | collective-permute-start | bytes 1572872 | tf_op jit(solution)/shard_map/while/body/eval_jaxpr/ppermute | solution.py:16
  146.8 10.7 %collective-permute-start = (bf16[512,512]{0,1:T(8,128)(2,1)}, bf16[512,512]{0,1:T(8,128)(2,1)S(1)}, u32[]{:S(2)}, u32[]{:S(2)}) collective-permute-start(bf16[512,512]{0,1:T(8,128)(2,1)} %get-tuple-element.290), channel_id=1, source_target_pairs={{0,4},{4,8},{8,12},{12,16},{16,20},{20,24},{24,28},{28,32},{32,36}... | collective-permute-start | bytes 1572872 | tf_op jit(solution)/shard_map/while/body/eval_jaxpr/ppermute | solution.py:16
  157.5 1.9 copy-start.5
  161.5 10.7 %collective-permute-start = (bf16[512,512]{0,1:T(8,128)(2,1)}, bf16[512,512]{0,1:T(8,128)(2,1)S(1)}, u32[]{:S(2)}, u32[]{:S(2)}) collective-permute-start(bf16[512,512]{0,1:T(8,128)(2,1)} %get-tuple-element.290), channel_id=1, source_target_pairs={{0,4},{4,8},{8,12},{12,16},{16,20},{20,24},{24,28},{28,32},{32,36}... | collective-permute-start | bytes 1572872 | tf_op jit(solution)/shard_map/while/body/eval_jaxpr/ppermute | solution.py:16
  176.2 10.7 %collective-permute-start = (bf16[512,512]{0,1:T(8,128)(2,1)}, bf16[512,512]{0,1:T(8,128)(2,1)S(1)}, u32[]{:S(2)}, u32[]{:S(2)}) collective-permute-start(bf16[512,512]{0,1:T(8,128)(2,1)} %get-tuple-element.290), channel_id=1, source_target_pairs={{0,4},{4,8},{8,12},{12,16},{16,20},{20,24},{24,28},{28,32},{32,36}... | collective-permute-start | bytes 1572872 | tf_op jit(solution)/shard_map/while/body/eval_jaxpr/ppermute | solution.py:16
  190.9 10.7 %collective-permute-start = (bf16[512,512]{0,1:T(8,128)(2,1)}, bf16[512,512]{0,1:T(8,128)(2,1)S(1)}, u32[]{:S(2)}, u32[]{:S(2)}) collective-permute-start(bf16[512,512]{0,1:T(8,128)(2,1)} %get-tuple-element.290), channel_id=1, source_target_pairs={{0,4},{4,8},{8,12},{12,16},{16,20},{20,24},{24,28},{28,32},{32,36}... | collective-permute-start | bytes 1572872 | tf_op jit(solution)/shard_map/while/body/eval_jaxpr/ppermute | solution.py:16
  205.6 10.7 %collective-permute-start = (bf16[512,512]{0,1:T(8,128)(2,1)}, bf16[512,512]{0,1:T(8,128)(2,1)S(1)}, u32[]{:S(2)}, u32[]{:S(2)}) collective-permute-start(bf16[512,512]{0,1:T(8,128)(2,1)} %get-tuple-element.290), channel_id=1, source_target_pairs={{0,4},{4,8},{8,12},{12,16},{16,20},{20,24},{24,28},{28,32},{32,36}... | collective-permute-start | bytes 1572872 | tf_op jit(solution)/shard_map/while/body/eval_jaxpr/ppermute | solution.py:16
  220.3 10.7 %collective-permute-start = (bf16[512,512]{0,1:T(8,128)(2,1)}, bf16[512,512]{0,1:T(8,128)(2,1)S(1)}, u32[]{:S(2)}, u32[]{:S(2)}) collective-permute-start(bf16[512,512]{0,1:T(8,128)(2,1)} %get-tuple-element.290), channel_id=1, source_target_pairs={{0,4},{4,8},{8,12},{12,16},{16,20},{20,24},{24,28},{28,32},{32,36}... | collective-permute-start | bytes 1572872 | tf_op jit(solution)/shard_map/while/body/eval_jaxpr/ppermute | solution.py:16
  234.9 10.7 %collective-permute-start = (bf16[512,512]{0,1:T(8,128)(2,1)}, bf16[512,512]{0,1:T(8,128)(2,1)S(1)}, u32[]{:S(2)}, u32[]{:S(2)}) collective-permute-start(bf16[512,512]{0,1:T(8,128)(2,1)} %get-tuple-element.290), channel_id=1, source_target_pairs={{0,4},{4,8},{8,12},{12,16},{16,20},{20,24},{24,28},{28,32},{32,36}... | collective-permute-start | bytes 1572872 | tf_op jit(solution)/shard_map/while/body/eval_jaxpr/ppermute | solution.py:16
  249.6 10.7 %collective-permute-start = (bf16[512,512]{0,1:T(8,128)(2,1)}, bf16[512,512]{0,1:T(8,128)(2,1)S(1)}, u32[]{:S(2)}, u32[]{:S(2)}) collective-permute-start(bf16[512,512]{0,1:T(8,128)(2,1)} %get-tuple-element.290), channel_id=1, source_target_pairs={{0,4},{4,8},{8,12},{12,16},{16,20},{20,24},{24,28},{28,32},{32,36}... | collective-permute-start | bytes 1572872 | tf_op jit(solution)/shard_map/while/body/eval_jaxpr/ppermute | solution.py:16
  264.3 10.7 %collective-permute-start = (bf16[512,512]{0,1:T(8,128)(2,1)}, bf16[512,512]{0,1:T(8,128)(2,1)S(1)}, u32[]{:S(2)}, u32[]{:S(2)}) collective-permute-start(bf16[512,512]{0,1:T(8,128)(2,1)} %get-tuple-element.290), channel_id=1, source_target_pairs={{0,4},{4,8},{8,12},{12,16},{16,20},{20,24},{24,28},{28,32},{32,36}... | collective-permute-start | bytes 1572872 | tf_op jit(solution)/shard_map/while/body/eval_jaxpr/ppermute | solution.py:16
  279.0 10.7 %collective-permute-start = (bf16[512,512]{0,1:T(8,128)(2,1)}, bf16[512,512]{0,1:T(8,128)(2,1)S(1)}, u32[]{:S(2)}, u32[]{:S(2)}) collective-permute-start(bf16[512,512]{0,1:T(8,128)(2,1)} %get-tuple-element.290), channel_id=1, source_target_pairs={{0,4},{4,8},{8,12},{12,16},{16,20},{20,24},{24,28},{28,32},{32,36}... | collective-permute-start | bytes 1572872 | tf_op jit(solution)/shard_map/while/body/eval_jaxpr/ppermute | solution.py:16
  293.7 10.7 %collective-permute-start = (bf16[512,512]{0,1:T(8,128)(2,1)}, bf16[512,512]{0,1:T(8,128)(2,1)S(1)}, u32[]{:S(2)}, u32[]{:S(2)}) collective-permute-start(bf16[512,512]{0,1:T(8,128)(2,1)} %get-tuple-element.290), channel_id=1, source_target_pairs={{0,4},{4,8},{8,12},{12,16},{16,20},{20,24},{24,28},{28,32},{32,36}... | collective-permute-start | bytes 1572872 | tf_op jit(solution)/shard_map/while/body/eval_jaxpr/ppermute | solution.py:16
  308.4 10.7 %collective-permute-start = (bf16[512,512]{0,1:T(8,128)(2,1)}, bf16[512,512]{0,1:T(8,128)(2,1)S(1)}, u32[]{:S(2)}, u32[]{:S(2)}) collective-permute-start(bf16[512,512]{0,1:T(8,128)(2,1)} %get-tuple-element.290), channel_id=1, source_target_pairs={{0,4},{4,8},{8,12},{12,16},{16,20},{20,24},{24,28},{28,32},{32,36}... | collective-permute-start | bytes 1572872 | tf_op jit(solution)/shard_map/while/body/eval_jaxpr/ppermute | solution.py:16
  (29 other events, 40.1 us)
Sparse Core Ops, SparseCore 0:
  9.8 63.1 all-gather.2
  325.0 164.9 all-gather.4
where the time goes:
time: 501 us; the launch traced here: 500 us
  waiting for transfers between devices  305 us (61%)
  starting transfers between devices  79.5 us (16%)
  matrix products  46.4 us (9%)
  other arithmetic  31.1 us (6%)
  local copies, waits for them, and re-layouts  22.4 us (4%)
  between operations  14.4 us (3%)
    all_gather x1, waiting for transfers between devices, body(): attended_all = lax.all_gather(attended, 'tp', axis=1, tiled=True)  158 us
    ppermute x17, waiting for transfers between devices, passed_along(): return lax.ppermute(x, axis, pairs)  95.9 us
    ppermute x17, starting transfers between devices, passed_along(): return lax.ppermute(x, axis, pairs)  73.1 us
    all_gather x1, waiting for transfers between devices, body(): gathered = lax.all_gather(residual, 'tp', axis=1, tiled=True)  50.8 us
    dot_general x17, matrix products, attend_block(): jnp.einsum('hqk,khd->qhd', weights.astype(jnp.bfloat16), key_value[:, :,...  19.7 us
    dot_general x17, matrix products, attend_block(): jnp.einsum('qhd,khd->hqk', queries, key_value[:, :, 0, :], preferred_elem...  17.8 us
    reduce_sum x17, other arithmetic, attend_block(): norm_sum = norm_sum * shrink + jnp.sum(weights, axis=2)  15.4 us
    while x90, local copies, waits for them, and re-layouts  14.6 us
  transfers between devices with their start and end apart: 20, of which 18 were waited for; matrix products, arithmetic and copies ran while one was open for 19% of the time, Pallas kernels for 0%

commit v1 on v0

--- a/solution.py
+++ b/solution.py
@@ -1,3 +1,4 @@
+import functools
 import jax
 import jax.numpy as jnp
 from jax import lax
@@ -8,6 +9,18 @@
 SPAN = 16
 THETA = 130000.0
 EPS = 1e-05
+
+
+def manage_zones(x_in, join_dim):
+    return jnp.concatenate(
+        lax.all_to_all(
+            jnp.stack([x_in] * lax.axis_size("tp")), axis_name="tp", split_axis=0, concat_axis=0
+        ),
+        axis=join_dim,
+    )
+
+
+view_ticks_on = functools.partial(manage_zones, join_dim=1)
 
 
 def passed_along(x, axis, by):
@@ -142,7 +155,7 @@
     pick = jnp.argmax(match.astype(jnp.int32), axis=1)
     found = jnp.any(match, axis=1)
     cache_pages = jnp.where(found[:, None, None], cand_pages[pick], jnp.zeros_like(cand_pages[:1]))
-    attended_all = lax.all_gather(attended, "tp", axis=1, tiled=True)
+    attended_all = view_ticks_on(attended)
     projected = jnp.dot(attended_all, out_cols, preferred_element_type=jnp.float32)
     hidden = (residual.astype(jnp.float32) + projected).astype(jnp.bfloat16)
     return (hidden, cache_pages)

time: 501 us -> 494 us (0.986)
  the two profiles are of different devices: /device:TPU:1 before, /device:TPU:128 now
where the time goes in v1:
time: 494 us; the launch traced here: 493 us
  waiting for transfers between devices  328 us (66%)
  starting transfers between devices  54.7 us (11%)
  matrix products  45.1 us (9%)
  other arithmetic  28.9 us (6%)
  local copies, waits for them, and re-layouts  20.2 us (4%)
  between operations  14.4 us (3%)
    ppermute x17, waiting for transfers between devices, passed_along(): return lax.ppermute(x, axis, pairs)  264 us
    all_gather x1, waiting for transfers between devices, body(): gathered = lax.all_gather(residual, 'tp', axis=1, tiled=True)  54.9 us
    ppermute x17, starting transfers between devices, passed_along(): return lax.ppermute(x, axis, pairs)  32.6 us
    dot_general x17, matrix products, attend_block(): jnp.einsum('hqk,khd->qhd', weights.astype(jnp.bfloat16), key_value[:, :,...  18.9 us
    all_to_all x1, starting transfers between devices, manage_zones(): lax.all_to_all(jnp.stack([x_in] * lax.axis_size('tp')), axis_name='tp', s...  17.8 us
    dot_general x17, matrix products, attend_block(): jnp.einsum('qhd,khd->hqk', queries, key_value[:, :, 0, :], preferred_elem...  17.3 us
    reduce_sum x17, other arithmetic, attend_block(): norm_sum = norm_sum * shrink + jnp.sum(weights, axis=2)  15.4 us
    while x30, local copies, waits for them, and re-layouts  12 us
  transfers between devices with their start and end apart: 20, of which 18 were waited for; matrix products, arithmetic and copies ran while one was open for 18% of the time, Pallas kernels for 0%

profile of v1, /device:TPU:128, one launch (start us, length us, event | category | flops | bytes accessed | tf_op | source)
XLA Modules:
  0.0 492.7 jit_solution(12582836617426620356)
XLA Ops:
  10.8 4.3 all-to-all-start.1
  15.0 1.9 collective-permute-start.2
  17.7 54.9 %all-gather.2.cloned.1.call-done = bf16[512,2048]{1,0:T(8,128)(2,1)} async-done(((bf16[512,512]{1,0:T(8,128)(2,1)}), bf16[512,2048]{1,0:T(8,128)(2,1)}) %all-gather.2.cloned.1.call-update) | async-done | bytes 2097168 | tf_op jit(solution)/shard_map/all_gather | solution.py:59
  72.6 2.2 fusion.17
  74.9 2.5 fusion.67
  77.4 2.3 fusion.64
  82.5 2.1 collective-permute-start.1
  88.0 13.5 %collective-permute-done.1 = bf16[512,512]{0,1:T(8,128)(2,1)S(1)} collective-permute-done((bf16[512,512]{0,1:T(8,128)(2,1)}, bf16[512,512]{0,1:T(8,128)(2,1)S(1)}, u32[]{:S(2)}, u32[]{:S(2)}) %collective-permute-start.1) | collective-permute-done | bytes 524320 | tf_op jit(solution)/shard_map/ppermute | solution.py:29
  101.4 1.9 select_reduce_fusion.1
  108.2 339.3 %while.20 = (s32[]{:T(128)}, bf16[512,512]{0,1:T(8,128)(2,1)}, f32[4,512]{1,0:T(4,128)S(1)}, f32[4,512]{1,0:T(4,128)S(1)}, f32[512,4,64]{0,2,1:T(8,128)S(1)}, /*...) while((s32[]{:T(128)}, bf16[512,512]{0,1:T(8,128)(2,1)}, ...), condition=%wide.region_8.9_spmd.clone, body=%wide.region_5.8_spmd.clone.sunk | while | flops 280500736 | bytes 18749628 | solution.py:139
  110.4 16.7 %collective-permute-done = bf16[512,512]{0,1:T(8,128)(2,1)S(1)} collective-permute-done((bf16[512,512]{0,1:T(8,128)(2,1)}, bf16[512,512]{0,1:T(8,128)(2,1)S(1)}, u32[]{:S(2)}, u32[]{:S(2)}) %collective-permute-start) | collective-permute-done | bytes 524320 | tf_op jit(solution)/shard_map/while/body/eval_jaxpr/ppermute | solution.py:29
  130.8 1.9 collective-permute-start
  133.0 16.7 %collective-permute-done = bf16[512,512]{0,1:T(8,128)(2,1)S(1)} collective-permute-done((bf16[512,512]{0,1:T(8,128)(2,1)}, bf16[512,512]{0,1:T(8,128)(2,1)S(1)}, u32[]{:S(2)}, u32[]{:S(2)}) %collective-permute-start) | collective-permute-done | bytes 524320 | tf_op jit(solution)/shard_map/while/body/eval_jaxpr/ppermute | solution.py:29
  155.6 16.7 %collective-permute-done = bf16[512,512]{0,1:T(8,128)(2,1)S(1)} collective-permute-done((bf16[512,512]{0,1:T(8,128)(2,1)}, bf16[512,512]{0,1:T(8,128)(2,1)S(1)}, u32[]{:S(2)}, u32[]{:S(2)}) %collective-permute-start) | collective-permute-done | bytes 524320 | tf_op jit(solution)/shard_map/while/body/eval_jaxpr/ppermute | solution.py:29
  176.1 1.9 collective-permute-start
  178.2 16.7 %collective-permute-done = bf16[512,512]{0,1:T(8,128)(2,1)S(1)} collective-permute-done((bf16[512,512]{0,1:T(8,128)(2,1)}, bf16[512,512]{0,1:T(8,128)(2,1)S(1)}, u32[]{:S(2)}, u32[]{:S(2)}) %collective-permute-start) | collective-permute-done | bytes 524320 | tf_op jit(solution)/shard_map/while/body/eval_jaxpr/ppermute | solution.py:29
  198.7 1.9 collective-permute-start
  200.8 16.7 %collective-permute-done = bf16[512,512]{0,1:T(8,128)(2,1)S(1)} collective-permute-done((bf16[512,512]{0,1:T(8,128)(2,1)}, bf16[512,512]{0,1:T(8,128)(2,1)S(1)}, u32[]{:S(2)}, u32[]{:S(2)}) %collective-permute-start) | collective-permute-done | bytes 524320 | tf_op jit(solution)/shard_map/while/body/eval_jaxpr/ppermute | solution.py:29
  221.3 1.9 collective-permute-start
  223.5 16.7 %collective-permute-done = bf16[512,512]{0,1:T(8,128)(2,1)S(1)} collective-permute-done((bf16[512,512]{0,1:T(8,128)(2,1)}, bf16[512,512]{0,1:T(8,128)(2,1)S(1)}, u32[]{:S(2)}, u32[]{:S(2)}) %collective-permute-start) | collective-permute-done | bytes 524320 | tf_op jit(solution)/shard_map/while/body/eval_jaxpr/ppermute | solution.py:29
  246.1 16.7 %collective-permute-done = bf16[512,512]{0,1:T(8,128)(2,1)S(1)} collective-permute-done((bf16[512,512]{0,1:T(8,128)(2,1)}, bf16[512,512]{0,1:T(8,128)(2,1)S(1)}, u32[]{:S(2)}, u32[]{:S(2)}) %collective-permute-start) | collective-permute-done | bytes 524320 | tf_op jit(solution)/shard_map/while/body/eval_jaxpr/ppermute | solution.py:29
  268.7 16.7 %collective-permute-done = bf16[512,512]{0,1:T(8,128)(2,1)S(1)} collective-permute-done((bf16[512,512]{0,1:T(8,128)(2,1)}, bf16[512,512]{0,1:T(8,128)(2,1)S(1)}, u32[]{:S(2)}, u32[]{:S(2)}) %collective-permute-start) | collective-permute-done | bytes 524320 | tf_op jit(solution)/shard_map/while/body/eval_jaxpr/ppermute | solution.py:29
  291.3 16.7 %collective-permute-done = bf16[512,512]{0,1:T(8,128)(2,1)S(1)} collective-permute-done((bf16[512,512]{0,1:T(8,128)(2,1)}, bf16[512,512]{0,1:T(8,128)(2,1)S(1)}, u32[]{:S(2)}, u32[]{:S(2)}) %collective-permute-start) | collective-permute-done | bytes 524320 | tf_op jit(solution)/shard_map/while/body/eval_jaxpr/ppermute | solution.py:29
  313.9 16.7 %collective-permute-done = bf16[512,512]{0,1:T(8,128)(2,1)S(1)} collective-permute-done((bf16[512,512]{0,1:T(8,128)(2,1)}, bf16[512,512]{0,1:T(8,128)(2,1)S(1)}, u32[]{:S(2)}, u32[]{:S(2)}) %collective-permute-start) | collective-permute-done | bytes 524320 | tf_op jit(solution)/shard_map/while/body/eval_jaxpr/ppermute | solution.py:29
  336.6 16.7 %collective-permute-done = bf16[512,512]{0,1:T(8,128)(2,1)S(1)} collective-permute-done((bf16[512,512]{0,1:T(8,128)(2,1)}, bf16[512,512]{0,1:T(8,128)(2,1)S(1)}, u32[]{:S(2)}, u32[]{:S(2)}) %collective-permute-start) | collective-permute-done | bytes 524320 | tf_op jit(solution)/shard_map/while/body/eval_jaxpr/ppermute | solution.py:29
  359.2 16.7 %collective-permute-done = bf16[512,512]{0,1:T(8,128)(2,1)S(1)} collective-permute-done((bf16[512,512]{0,1:T(8,128)(2,1)}, bf16[512,512]{0,1:T(8,128)(2,1)S(1)}, u32[]{:S(2)}, u32[]{:S(2)}) %collective-permute-start) | collective-permute-done | bytes 524320 | tf_op jit(solution)/shard_map/while/body/eval_jaxpr/ppermute | solution.py:29
  381.8 16.7 %collective-permute-done = bf16[512,512]{0,1:T(8,128)(2,1)S(1)} collective-permute-done((bf16[512,512]{0,1:T(8,128)(2,1)}, bf16[512,512]{0,1:T(8,128)(2,1)S(1)}, u32[]{:S(2)}, u32[]{:S(2)}) %collective-permute-start) | collective-permute-done | bytes 524320 | tf_op jit(solution)/shard_map/while/body/eval_jaxpr/ppermute | solution.py:29
  404.4 16.7 %collective-permute-done = bf16[512,512]{0,1:T(8,128)(2,1)S(1)} collective-permute-done((bf16[512,512]{0,1:T(8,128)(2,1)}, bf16[512,512]{0,1:T(8,128)(2,1)S(1)}, u32[]{:S(2)}, u32[]{:S(2)}) %collective-permute-start) | collective-permute-done | bytes 524320 | tf_op jit(solution)/shard_map/while/body/eval_jaxpr/ppermute | solution.py:29
  427.0 16.7 %collective-permute-done = bf16[512,512]{0,1:T(8,128)(2,1)S(1)} collective-permute-done((bf16[512,512]{0,1:T(8,128)(2,1)}, bf16[512,512]{0,1:T(8,128)(2,1)S(1)}, u32[]{:S(2)}, u32[]{:S(2)}) %collective-permute-start) | collective-permute-done | bytes 524320 | tf_op jit(solution)/shard_map/while/body/eval_jaxpr/ppermute | solution.py:29
  448.8 17.8 %all-to-all-start = ((bf16[4,512,256]{2,1,0:T(8,128)(2,1)}), bf16[4,512,256]{2,1,0:T(8,128)(2,1)}, u32[]{:S(2)}, u32[]{:S(2)}) async-start(bf16[4,512,256]{2,1,0:T(8,128)(2,1)} %stack.3), calls=%async_computation | async-start | bytes 2097152 | tf_op jit(solution)/shard_map/all_to_all | solution.py:16
  473.4 9.2 %all-to-all-done = bf16[4,512,256]{2,1,0:T(8,128)(2,1)} async-done(((bf16[4,512,256]{2,1,0:T(8,128)(2,1)}), bf16[4,512,256]{2,1,0:T(8,128)(2,1)}, u32[]{:S(2)}, u32[]{:S(2)}) %all-to-all-start) | async-done | bytes 1048608 | tf_op jit(solution)/shard_map/all_to_all | solution.py:16
  482.6 3.2 fusion.31
  (207 shorter events, 103.8 us)
Async XLA Ops:
  7.2 67.7 %copy-start = (bf16[2048,256]{1,0:T(8,128)(2,1)S(1)}, bf16[2048,256]{1,0:T(8,128)(2,1)}, u32[]{:S(2)}) copy-start(bf16[2048,256]{1,0:T(8,128)(2,1)} %param.14) | copy-start | bytes 3145732
  7.2 9.8 %copy-start.4 = (s32[512]{0:T(512)S(1)}, s32[512]{0:T(512)}, u32[]{:S(2)}) copy-start(s32[512]{0:T(512)} %param.18) | copy-start | bytes 6148
  7.2 9.8 %copy-start.3 = (s32[512]{0:T(512)S(1)}, s32[512]{0:T(512)}, u32[]{:S(2)}) copy-start(s32[512]{0:T(512)} %param.17) | copy-start | bytes 6148
  7.2 65.4 %all-gather.2.cloned.1.call-start = ((), (), s32[]{:S(2)}) async-start(), calls=%async_computation.2 | async-start | bytes 2621440 | tf_op jit(solution)/shard_map/all_gather | solution.py:59
  7.9 66.9 %copy-start.7 = (f32[2048]{0:T(1024)S(1)}, f32[2048]{0:T(1024)}, u32[]{:S(2)}) copy-start(f32[2048]{0:T(1024)} %param.12) | copy-start | bytes 24580
  10.8 436.9 %all-to-all-start.1 = ((bf16[256,4,512]{2,0,1:T(8,128)(2,1)}), bf16[256,4,512]{2,0,1:T(8,128)(2,1)}, u32[]{:S(2)}, u32[]{:S(2)}) async-start(bf16[256,4,512]{2,0,1:T(8,128)(2,1)} %copy.39), calls=%async_computation.1 | async-start | bytes 2097152 | tf_op jit(solution)/shard_map/all_to_all | solution.py:85
  15.0 451.6 %collective-permute-start.2 = (s32[4]{0:T(128)}, s32[4]{0:T(128)}, u32[]{:S(2)}, u32[]{:S(2)}) collective-permute-start(s32[4]{0:T(128)} %param.19), channel_id=1, source_target_pairs={{0,4},{4,8},{8,12},{12,16},{16,20},{20,24},{24,28},{28,32},{32,36}... | collective-permute-start | bytes 56 | tf_op jit(solution)/shard_map/ppermute | solution.py:29
  72.6 4.8 copy-start.1
  77.4 3.1 copy-start.6
  82.5 18.9 %collective-permute-start.1 = (bf16[512,512]{0,1:T(8,128)(2,1)}, bf16[512,512]{0,1:T(8,128)(2,1)S(1)}, u32[]{:S(2)}, u32[]{:S(2)}) collective-permute-start(bf16[512,512]{0,1:T(8,128)(2,1)} %bitcast_select_fusion), channel_id=1, source_target_pairs={{0,4},{4,8},{8,12},{12,16},{16,20},{20,24},{24,28},{28,32},{32,36}... | collective-permute-start | bytes 1572872 | tf_op jit(solution)/shard_map/ppermute | solution.py:29
  101.4 6.0 %copy-start.2 = (bf16[512,512]{0,1:T(8,128)(2,1)}, bf16[512,512]{0,1:T(8,128)(2,1)S(1)}, u32[]{:S(2)}) copy-start(bf16[512,512]{0,1:T(8,128)(2,1)S(1)} %collective-permute-done.1) | copy-start | bytes 1572868
  108.2 18.8 %collective-permute-start = (bf16[512,512]{0,1:T(8,128)(2,1)}, bf16[512,512]{0,1:T(8,128)(2,1)S(1)}, u32[]{:S(2)}, u32[]{:S(2)}) collective-permute-start(bf16[512,512]{0,1:T(8,128)(2,1)} %get-tuple-element.290), channel_id=1, source_target_pairs={{0,4},{4,8},{8,12},{12,16},{16,20},{20,24},{24,28},{28,32},{32,36}... | collective-permute-start | bytes 1572872 | tf_op jit(solution)/shard_map/while/body/eval_jaxpr/ppermute | solution.py:29
  130.8 18.8 %collective-permute-start = (bf16[512,512]{0,1:T(8,128)(2,1)}, bf16[512,512]{0,1:T(8,128)(2,1)S(1)}, u32[]{:S(2)}, u32[]{:S(2)}) collective-permute-start(bf16[512,512]{0,1:T(8,128)(2,1)} %get-tuple-element.290), channel_id=1, source_target_pairs={{0,4},{4,8},{8,12},{12,16},{16,20},{20,24},{24,28},{28,32},{32,36}... | collective-permute-start | bytes 1572872 | tf_op jit(solution)/shard_map/while/body/eval_jaxpr/ppermute | solution.py:29
  153.4 18.8 %collective-permute-start = (bf16[512,512]{0,1:T(8,128)(2,1)}, bf16[512,512]{0,1:T(8,128)(2,1)S(1)}, u32[]{:S(2)}, u32[]{:S(2)}) collective-permute-start(bf16[512,512]{0,1:T(8,128)(2,1)} %get-tuple-element.290), channel_id=1, source_target_pairs={{0,4},{4,8},{8,12},{12,16},{16,20},{20,24},{24,28},{28,32},{32,36}... | collective-permute-start | bytes 1572872 | tf_op jit(solution)/shard_map/while/body/eval_jaxpr/ppermute | solution.py:29
  176.1 18.8 %collective-permute-start = (bf16[512,512]{0,1:T(8,128)(2,1)}, bf16[512,512]{0,1:T(8,128)(2,1)S(1)}, u32[]{:S(2)}, u32[]{:S(2)}) collective-permute-start(bf16[512,512]{0,1:T(8,128)(2,1)} %get-tuple-element.290), channel_id=1, source_target_pairs={{0,4},{4,8},{8,12},{12,16},{16,20},{20,24},{24,28},{28,32},{32,36}... | collective-permute-start | bytes 1572872 | tf_op jit(solution)/shard_map/while/body/eval_jaxpr/ppermute | solution.py:29
  198.7 18.8 %collective-permute-start = (bf16[512,512]{0,1:T(8,128)(2,1)}, bf16[512,512]{0,1:T(8,128)(2,1)S(1)}, u32[]{:S(2)}, u32[]{:S(2)}) collective-permute-start(bf16[512,512]{0,1:T(8,128)(2,1)} %get-tuple-element.290), channel_id=1, source_target_pairs={{0,4},{4,8},{8,12},{12,16},{16,20},{20,24},{24,28},{28,32},{32,36}... | collective-permute-start | bytes 1572872 | tf_op jit(solution)/shard_map/while/body/eval_jaxpr/ppermute | solution.py:29
  221.3 18.8 %collective-permute-start = (bf16[512,512]{0,1:T(8,128)(2,1)}, bf16[512,512]{0,1:T(8,128)(2,1)S(1)}, u32[]{:S(2)}, u32[]{:S(2)}) collective-permute-start(bf16[512,512]{0,1:T(8,128)(2,1)} %get-tuple-element.290), channel_id=1, source_target_pairs={{0,4},{4,8},{8,12},{12,16},{16,20},{20,24},{24,28},{28,32},{32,36}... | collective-permute-start | bytes 1572872 | tf_op jit(solution)/shard_map/while/body/eval_jaxpr/ppermute | solution.py:29
  243.9 18.8 %collective-permute-start = (bf16[512,512]{0,1:T(8,128)(2,1)}, bf16[512,512]{0,1:T(8,128)(2,1)S(1)}, u32[]{:S(2)}, u32[]{:S(2)}) collective-permute-start(bf16[512,512]{0,1:T(8,128)(2,1)} %get-tuple-element.290), channel_id=1, source_target_pairs={{0,4},{4,8},{8,12},{12,16},{16,20},{20,24},{24,28},{28,32},{32,36}... | collective-permute-start | bytes 1572872 | tf_op jit(solution)/shard_map/while/body/eval_jaxpr/ppermute | solution.py:29
  266.5 18.8 %collective-permute-start = (bf16[512,512]{0,1:T(8,128)(2,1)}, bf16[512,512]{0,1:T(8,128)(2,1)S(1)}, u32[]{:S(2)}, u32[]{:S(2)}) collective-permute-start(bf16[512,512]{0,1:T(8,128)(2,1)} %get-tuple-element.290), channel_id=1, source_target_pairs={{0,4},{4,8},{8,12},{12,16},{16,20},{20,24},{24,28},{28,32},{32,36}... | collective-permute-start | bytes 1572872 | tf_op jit(solution)/shard_map/while/body/eval_jaxpr/ppermute | solution.py:29
  289.2 18.8 %collective-permute-start = (bf16[512,512]{0,1:T(8,128)(2,1)}, bf16[512,512]{0,1:T(8,128)(2,1)S(1)}, u32[]{:S(2)}, u32[]{:S(2)}) collective-permute-start(bf16[512,512]{0,1:T(8,128)(2,1)} %get-tuple-element.290), channel_id=1, source_target_pairs={{0,4},{4,8},{8,12},{12,16},{16,20},{20,24},{24,28},{28,32},{32,36}... | collective-permute-start | bytes 1572872 | tf_op jit(solution)/shard_map/while/body/eval_jaxpr/ppermute | solution.py:29
  311.8 18.8 %collective-permute-start = (bf16[512,512]{0,1:T(8,128)(2,1)}, bf16[512,512]{0,1:T(8,128)(2,1)S(1)}, u32[]{:S(2)}, u32[]{:S(2)}) collective-permute-start(bf16[512,512]{0,1:T(8,128)(2,1)} %get-tuple-element.290), channel_id=1, source_target_pairs={{0,4},{4,8},{8,12},{12,16},{16,20},{20,24},{24,28},{28,32},{32,36}... | collective-permute-start | bytes 1572872 | tf_op jit(solution)/shard_map/while/body/eval_jaxpr/ppermute | solution.py:29
  334.4 18.8 %collective-permute-start = (bf16[512,512]{0,1:T(8,128)(2,1)}, bf16[512,512]{0,1:T(8,128)(2,1)S(1)}, u32[]{:S(2)}, u32[]{:S(2)}) collective-permute-start(bf16[512,512]{0,1:T(8,128)(2,1)} %get-tuple-element.290), channel_id=1, source_target_pairs={{0,4},{4,8},{8,12},{12,16},{16,20},{20,24},{24,28},{28,32},{32,36}... | collective-permute-start | bytes 1572872 | tf_op jit(solution)/shard_map/while/body/eval_jaxpr/ppermute | solution.py:29
  357.0 18.8 %collective-permute-start = (bf16[512,512]{0,1:T(8,128)(2,1)}, bf16[512,512]{0,1:T(8,128)(2,1)S(1)}, u32[]{:S(2)}, u32[]{:S(2)}) collective-permute-start(bf16[512,512]{0,1:T(8,128)(2,1)} %get-tuple-element.290), channel_id=1, source_target_pairs={{0,4},{4,8},{8,12},{12,16},{16,20},{20,24},{24,28},{28,32},{32,36}... | collective-permute-start | bytes 1572872 | tf_op jit(solution)/shard_map/while/body/eval_jaxpr/ppermute | solution.py:29
  379.6 18.8 %collective-permute-start = (bf16[512,512]{0,1:T(8,128)(2,1)}, bf16[512,512]{0,1:T(8,128)(2,1)S(1)}, u32[]{:S(2)}, u32[]{:S(2)}) collective-permute-start(bf16[512,512]{0,1:T(8,128)(2,1)} %get-tuple-element.290), channel_id=1, source_target_pairs={{0,4},{4,8},{8,12},{12,16},{16,20},{20,24},{24,28},{28,32},{32,36}... | collective-permute-start | bytes 1572872 | tf_op jit(solution)/shard_map/while/body/eval_jaxpr/ppermute | solution.py:29
  402.3 18.8 %collective-permute-start = (bf16[512,512]{0,1:T(8,128)(2,1)}, bf16[512,512]{0,1:T(8,128)(2,1)S(1)}, u32[]{:S(2)}, u32[]{:S(2)}) collective-permute-start(bf16[512,512]{0,1:T(8,128)(2,1)} %get-tuple-element.290), channel_id=1, source_target_pairs={{0,4},{4,8},{8,12},{12,16},{16,20},{20,24},{24,28},{28,32},{32,36}... | collective-permute-start | bytes 1572872 | tf_op jit(solution)/shard_map/while/body/eval_jaxpr/ppermute | solution.py:29
  424.9 18.8 %collective-permute-start = (bf16[512,512]{0,1:T(8,128)(2,1)}, bf16[512,512]{0,1:T(8,128)(2,1)S(1)}, u32[]{:S(2)}, u32[]{:S(2)}) collective-permute-start(bf16[512,512]{0,1:T(8,128)(2,1)} %get-tuple-element.290), channel_id=1, source_target_pairs={{0,4},{4,8},{8,12},{12,16},{16,20},{20,24},{24,28},{28,32},{32,36}... | collective-permute-start | bytes 1572872 | tf_op jit(solution)/shard_map/while/body/eval_jaxpr/ppermute | solution.py:29
  447.5 22.7 %copy-start.5 = (pred[4,128]{1,0:T(4,128)(4,1)S(1)}, pred[4,128]{1,0:T(4,128)(4,1)}, u32[]{:S(2)}) copy-start(pred[4,128]{1,0:T(4,128)(4,1)} %fusion.73) | copy-start | bytes 1540
  448.8 33.8 %all-to-all-start = ((bf16[4,512,256]{2,1,0:T(8,128)(2,1)}), bf16[4,512,256]{2,1,0:T(8,128)(2,1)}, u32[]{:S(2)}, u32[]{:S(2)}) async-start(bf16[4,512,256]{2,1,0:T(8,128)(2,1)} %stack.3), calls=%async_computation | async-start | bytes 2097152 | tf_op jit(solution)/shard_map/all_to_all | solution.py:16
Sparse Core Ops, SparseCore 0:
  9.8 62.7 all-gather.1
